TPU v7x, 32 devices: a whole 2x2x4 slice. The times are simulated.
32 devices in a mesh: groups: 2 (over y), blk: 4 (over z), pool: 4 (over x, core).
Axes of the slice: x: 2, y: 2, z: 4, core: 2. Of those that a mesh axis runs over, the one named last changes fastest.
Arguments:
- q_new: bfloat16 [1024, 8192], P(('groups', 'blk'), 'pool'), parts along dimension 0, may hold values from -64 to 64
- kv_new: bfloat16 [1024, 8, 256], P(('groups', 'blk'), 'pool'), parts along dimension 0, may hold values from -7 to 7
- kv_cache: bfloat16 [256, 8, 128, 256], P(('groups', 'blk'), 'pool'), parts along dimension 0, may hold values from -4.5 to 4.5
- page_table: int32 [16], P('groups'), parts along dimension 0, may hold values from 0 to 127, as said below
- block_offsets: int32 [8], P('groups'), parts along dimension 0, may hold values from 0 to 3, each once
Outputs:
- attended: bfloat16 [1024, 8192], P(('groups', 'blk'), 'pool'), parts along dimension 0
There are 2 independent parts, one for each index of `groups`. A program takes and returns all parts, laid end to end along the dimension named above; each array names one. Nothing has to cross between parts.
Inputs may be any that keep to these rules, and one draw needn't show every extreme that they name: `page_table`: distinct slots; slot s lies on blk index s // 32; at most 4 entries lie on the slots of one blk index, and exactly 4 on some blk index.
All inputs are finite; a program needn't handle non-finite values.
Results may differ from a plain program's by a relative error of at most 0.0045.
Values may be sent and summed in bfloat16 or wider, within the bound.
No kernel may reach another device: no remote copies, remote signals or barrier semaphores. Data moves between devices by JAX's collectives and lax.ppermute only.
A program may use at most 64 MiB of HBM per device.

v0:
```python
import math
import jax
import jax.numpy as jnp
from jax import lax
from jax.sharding import PartitionSpec as P

CAP = 4


def attend(running, queries, keys, values, visible, head_size):
    maxima, totals, summed = running
    score_scale = 1.0 / math.sqrt(head_size)
    scores = (
        jnp.einsum("gqd,gkd->gqk", queries, keys, preferred_element_type=jnp.float32) * score_scale
    )
    scores = jnp.where(visible, scores, -1e30)
    row_top = jnp.maximum(maxima, jnp.max(scores, axis=2))
    factor = jnp.exp(maxima - row_top)
    weights = jnp.where(visible, jnp.exp(scores - row_top[..., None]), 0.0)
    totals = totals * factor + jnp.sum(weights, axis=2)
    summed = summed * factor[..., None] + jnp.einsum(
        "gqk,gkd->gqd", weights.astype(jnp.bfloat16), values, preferred_element_type=jnp.float32
    )
    return (row_top, totals, summed)


def local(q_new, kv_new, kv_cache, page_table, block_offsets):
    q_rows = q_new.shape[0]
    kv_heads = kv_new.shape[1]
    head_size = kv_new.shape[2] // 2
    group_size = q_new.shape[1] // (head_size * kv_heads)
    slots_dev = kv_cache.shape[0]
    page_len = kv_cache.shape[2]
    npages = page_table.shape[0]
    blocks = lax.axis_size("blk")
    myself = lax.axis_index("blk")
    pg = -(-npages // blocks)
    block_ids = jnp.arange(blocks, dtype=jnp.int32)
    my_offset = jnp.sum(jnp.where(block_ids == myself, block_offsets, 0))
    query_pos = jnp.tile(my_offset * q_rows + jnp.arange(q_rows, dtype=jnp.int32), group_size)
    queries = (
        q_new.reshape(q_rows, kv_heads, group_size, head_size)
        .transpose(1, 2, 0, 3)
        .reshape(kv_heads, group_size * q_rows, head_size)
    )
    query_span = group_size * q_rows
    new_all = lax.all_gather(kv_new.transpose(1, 0, 2), "blk", axis=0)
    page_owner = page_table // slots_dev
    owned = page_owner == myself
    page_rank = jnp.cumsum(owned.astype(jnp.int32)) - 1
    local_slot = page_table % slots_dev
    counts = jnp.sum((page_owner[None, :] == block_ids[:, None]).astype(jnp.int32), axis=1)
    per_peer = (CAP + blocks - 1) // blocks
    starts = jnp.cumsum(counts) - counts
    my_start = jnp.sum(jnp.where(block_ids == myself, starts, 0))
    peer_slots = jnp.arange(per_peer, dtype=jnp.int32)[None, :]
    wanted = (block_ids[:, None] - my_start) % blocks + peer_slots * blocks
    picked = owned[None, None, :] & (page_rank[None, None, :] == wanted[..., None])
    chosen = jnp.sum(jnp.where(picked, local_slot[None, None, :], 0), axis=2).reshape(-1)
    sent_pages = kv_cache[chosen].reshape(blocks, per_peer, kv_heads, page_len, 2 * head_size)
    sent_pages = sent_pages.transpose(0, 2, 1, 3, 4).reshape(
        blocks, kv_heads, per_peer * page_len, 2 * head_size
    )
    received = lax.all_to_all(sent_pages, "blk", split_axis=0, concat_axis=0, tiled=True)
    page_part = received[:, :, : per_peer * page_len]
    page_part = page_part.reshape(blocks, kv_heads, per_peer, page_len, 2 * head_size)
    page_part = page_part.transpose(0, 2, 1, 3, 4).reshape(
        blocks * per_peer, kv_heads, page_len, 2 * head_size
    )
    arriving = (myself - starts[:, None]) % blocks + peer_slots * blocks
    present = (arriving < counts[:, None]).reshape(-1)
    order_rank = jnp.cumsum(present.astype(jnp.int32)) - 1
    choose = present[None, :] & (order_rank[None, :] == jnp.arange(pg, dtype=jnp.int32)[:, None])
    positions = jnp.sum(
        jnp.where(choose, jnp.arange(blocks * per_peer, dtype=jnp.int32)[None, :], 0), axis=1
    )
    compact = page_part[positions]
    compact_valid = jnp.arange(pg, dtype=jnp.int32) * blocks + myself < npages
    gathered = lax.all_gather(compact, "blk", axis=0, tiled=True)
    gathered_valid = (
        jnp.arange(pg, dtype=jnp.int32)[None, :] * blocks + block_ids[:, None] < npages
    ).reshape(-1)
    new_rows = new_all.transpose(1, 0, 2, 3).reshape(kv_heads, blocks * q_rows, 2 * head_size)
    own_pages = compact.transpose(1, 0, 2, 3).reshape(kv_heads, pg * page_len, 2 * head_size)
    entries_a = jnp.concatenate([new_rows, own_pages], axis=1)
    row_source = jnp.repeat(block_ids, q_rows)
    key_pos = jnp.sum(
        jnp.where(row_source[:, None] == block_ids[None, :], block_offsets[None, :], 0), axis=1
    ) * q_rows + jnp.tile(jnp.arange(q_rows, dtype=jnp.int32), blocks)
    visible_new = key_pos[None, :] <= query_pos[:, None]
    visible_own = jnp.broadcast_to(
        jnp.repeat(compact_valid, page_len)[None, :], (query_span, pg * page_len)
    )
    visible_a = jnp.concatenate([visible_new, visible_own], axis=1)[None]
    running = (
        jnp.full((kv_heads, query_span), -1e30, jnp.float32),
        jnp.zeros((kv_heads, query_span), jnp.float32),
        jnp.zeros((kv_heads, query_span, head_size), jnp.float32),
    )
    running = attend(
        running,
        queries,
        entries_a[..., :head_size],
        entries_a[..., head_size:],
        visible_a,
        head_size,
    )
    page_block = jnp.repeat(block_ids, pg)
    use_page = gathered_valid & (page_block != myself)
    entries_b = gathered.transpose(1, 0, 2, 3).reshape(
        kv_heads, blocks * pg * page_len, 2 * head_size
    )
    visible_b = jnp.repeat(use_page, page_len)[None, None, :]
    running = attend(
        running,
        queries,
        entries_b[..., :head_size],
        entries_b[..., head_size:],
        visible_b,
        head_size,
    )
    maxima, totals, summed = running
    attended = (summed / totals[..., None]).astype(jnp.bfloat16)
    attended = attended.reshape(kv_heads, group_size, q_rows, head_size).transpose(2, 0, 1, 3)
    return attended.reshape(q_rows, kv_heads * group_size * head_size)


def solution(mesh):
    return jax.shard_map(
        local,
        mesh=mesh,
        in_specs=(
            P(("groups", "blk"), "pool"),
            P(("groups", "blk"), "pool", None),
            P(("groups", "blk"), "pool", None, None),
            P("groups"),
            P("groups"),
        ),
        out_specs=P(("groups", "blk"), "pool"),
        check_vma=False,
    )
```

profile of v0, /device:TPU:0, one launch (start us, length us, event | category | flops | bytes accessed | tf_op | source)
XLA Modules:
  0.0 99.0 jit_solution(9851125789988168862)
XLA Ops:
  6.5 0.7 and_select_fusion.3
  7.2 0.7 convert_bitcast_fusion
  8.3 1.4 %fusion.35 = (s32[]{:T(128)}, s32[]{:T(128)}) fusion(s32[4]{0:T(128)} %param.9, s32[]{:T(128)S(6)} %axis_index.15, s32[4]{0:T(128)S(1)} %convert_reduce_fusion, s32[4,1]{0,1:T(1,128)S(1)} %reduce-window.22), kind=kLoop, calls=%fused_computation.77 | loop fusion | flops 22 | bytes 60 | tf_op jit(solution)/shard_map/reduce_sum | solution.py:39
  9.7 0.7 and_select_fusion.4
  10.6 3.6 %gather_fusion = bf16[4,2,128,256]{3,2,1,0:T(8,128)(2,1)} fusion(bf16[32,2,128,256]{3,2,1,0:T(8,128)(2,1)} %param.7, s32[1024]{0:T(1024)S(1)} %pad_clamp_fusion.1), kind=kCustom, calls=%fused_computation | custom fusion | bytes 1048592 | tf_op jit(solution)/shard_map/gather | solution.py:60
  14.1 6.3 %all-to-all-start = ((bf16[4,2,128,256]{3,2,1,0:T(8,128)(2,1)}), bf16[4,2,128,256]{3,2,1,0:T(8,128)(2,1)S(1)}, u32[]{:S(2)}, u32[]{:S(2)}) async-start(bf16[4,2,128,256]{3,2,1,0:T(8,128)(2,1)} %gather_fusion), calls=%async_computation | async-start | bytes 1048576 | tf_op jit(solution)/shard_map/all_to_all | solution.py:64
  21.6 0.9 copy.36
  22.5 22.7 %all-gather = bf16[8,128,256]{2,1,0:T(8,128)(2,1)S(1)} all-gather(bf16[2,128,256]{2,1,0:T(8,128)(2,1)S(1)} %bitcast.101), channel_id=2, replica_groups=mesh['groups'=2,'blk'=4,'pool'=4] {'blk'}, dimensions={0}, use_global_device_ids=true | all-gather | bytes 655360 | tf_op jit(solution)/shard_map/all_gather | solution.py:47
  45.3 1.1 %copy.31 = bf16[16,8,16,128]{3,2,1,0:T(8,128)(2,1)S(1)} copy(bf16[16,8,16,128]{3,1,2,0:T(8,128)(2,1)} %bitcast.102) | data formatting | bytes 1048576
  46.8 0.7 select_reduce_fusion
  47.5 1.3 %gather_fusion.1 = bf16[2,2,128,256]{3,2,1,0:T(8,128)(2,1)} fusion(bf16[4,2,128,256]{3,2,1,0:T(8,128)(2,1)S(1)} %all-to-all-done, s32[1024]{0:T(1024)S(1)} %pad_clamp_fusion), kind=kCustom, calls=%fused_computation.1 | custom fusion | bytes 524296 | tf_op jit(solution)/shard_map/gather | solution.py:77
  48.9 0.4 broadcast_compare_fusion
  49.2 0.4 pad_add_fusion
  49.7 1.0 copy.23
  50.6 4.0 %fusion.4 = (f32[2,1024]{1,0:T(2,128)S(1)}, f32[2,768,1024]{2,1,0:T(8,128)}) fusion(pred[1024,768]{0,1:T(8,128)(4,1)S(1)} %pad_add_fusion, bf16[2,1024,128]{2,1,0:T(8,128)(2,1)S(1)} %bitcast.95, bf16[2,512,256]{2,1,0:T(8,128)(2,1)S(1)} %bitcast.103, bf16[2,256,256]{2,1,0:T(8,128)(2,1)S(1)} %bitcast.106), kind=kOutput, calls=%fused_computation.11 | convolution fusion | flops 408156160 | bytes 8396800 | tf_op jit(solution)/shard_map/gqd,gkd->gqk/dot_general | solution.py:14
  54.7 23.0 %all-gather.4.cloned.1.call-done = bf16[8,2,128,256]{3,2,1,0:T(8,128)(2,1)} async-done(((bf16[2,2,128,256]{3,2,1,0:T(8,128)(2,1)}), bf16[8,2,128,256]{3,2,1,0:T(8,128)(2,1)}) %all-gather.4.cloned.1.call-update) | async-done | bytes 1048592 | tf_op jit(solution)/shard_map/all_gather | solution.py:79
  77.7 1.3 %copy.26 = bf16[2,8,128,256]{3,2,1,0:T(8,128)(2,1)S(1)} copy(bf16[2,8,128,256]{3,2,0,1:T(8,128)(2,1)} %bitcast.100) | data formatting | bytes 2097152 | tf_op jit(solution)/shard_map/transpose | solution.py:110
  79.0 1.9 %bitcast_reduce_fusion = (f32[2,1024]{1,0:T(2,128)S(1)}, f32[2,1024,1024]{2,1,0:T(8,128)S(1)}) fusion(pred[1024]{0:T(1024)(128)(4,1)S(1)} %broadcast_bitcast_fusion.1, bf16[2,1024,128]{2,1,0:T(8,128)(2,1)S(1)} %bitcast.96, bf16[2,1024,256]{2,1,0:T(8,128)(2,1)S(1)} %bitcast.92), kind=kOutput, calls=%fused_computation.3 | convolution fusion | flops 543160320 | bytes 9446400 | tf_op jit(solution)/shard_map/gqd,gkd->gqk/dot_general | solution.py:14
  80.9 2.5 %fusion.2 = f32[2,1024]{1,0:T(2,128)S(1)} fusion(f32[2,1024,1024]{2,1,0:T(8,128)S(1)} %get-tuple-element.16, f32[2,1024]{1,0:T(2,128)S(1)} %get-tuple-element.11, pred[1024]{0:T(1024)(128)(4,1)S(1)} %broadcast_bitcast_fusion.1), kind=kLoop, calls=%fused_computation.9 | loop fusion | flops 10483712 | bytes 8406016 | tf_op jit(solution)/shard_map/reduce_sum | solution.py:20
  83.5 1.7 %fusion.5 = f32[2,1024]{1,0:T(2,128)S(1)} fusion(f32[2,768,1024]{2,1,0:T(8,128)S(1)} %bitcast.91, f32[2,1024]{1,0:T(2,128)S(1)} %get-tuple-element.12, pred[1024,768]{0,1:T(8,128)(4,1)S(1)} %pad_add_fusion), kind=kLoop, calls=%fused_computation.12 | loop fusion | flops 7862272 | bytes 7094272 | tf_op jit(solution)/shard_map/reduce_sum | solution.py:20
  85.1 2.8 %fusion.20 = f32[2,1024,128]{2,1,0:T(8,128)S(1)} fusion(f32[2,768,1024]{2,1,0:T(8,128)S(1)} %bitcast.91, f32[2,1024]{1,0:T(2,128)S(1)} %get-tuple-element.12, pred[1024,768]{0,1:T(8,128)(4,1)S(1)} %pad_add_fusion, f32[2,1024]{1,0:T(2,128)S(1)} %get-tuple-element.6, f32[2,1024]{1,0:T(2,128)S(1)} %get-tuple-element.10, ...), kind=kOutput, calls=%fused_computation.22 | convolution fusion | flops 411828224 | bytes 8937472 | tf_op jit(solution)/shard_map/gqk,gkd->gqd/dot_general | solution.py:21
  88.0 3.0 %divide_convert_fusion = bf16[2,1024,128]{2,1,0:T(8,128)(2,1)S(1)} fusion(f32[2,1024,128]{2,1,0:T(8,128)S(1)} %fusion.20, f32[2,1024,1024]{2,1,0:T(8,128)S(1)} %get-tuple-element.16, f32[2,1024]{1,0:T(2,128)S(1)} %get-tuple-element.11, pred[1024]{0:T(1024)(128)(4,1)S(1)} %broadcast_bitcast_fusion.1, bf16[2,1024,256]{2,1,0:T(8,128)(2,1)S(1)} %bitcast.93, ...), kind=kOutput, calls=%fused_computation.23 | convolution fusion | flops 548143104 | bytes 10504192 | tf_op jit(solution)/shard_map/gqk,gkd->gqd/dot_general | solution.py:21
  90.9 0.3 copy.28
  91.3 0.9 copy.35
  (37 shorter events, 1.6 us)
Async XLA Ops:
  14.1 33.4 %all-to-all-start = ((bf16[4,2,128,256]{3,2,1,0:T(8,128)(2,1)}), bf16[4,2,128,256]{3,2,1,0:T(8,128)(2,1)S(1)}, u32[]{:S(2)}, u32[]{:S(2)}) async-start(bf16[4,2,128,256]{3,2,1,0:T(8,128)(2,1)} %gather_fusion), calls=%async_computation | async-start | bytes 1048576 | tf_op jit(solution)/shard_map/all_to_all | solution.py:64
  20.5 57.2 %all-gather.4.cloned.1.call-start = ((), (), s32[]{:S(2)}) async-start(), calls=%async_computation.1 | async-start | bytes 1310720 | tf_op jit(solution)/shard_map/all_gather | solution.py:79
  79.0 4.4 %slice-start = ((s8[6291456]{0:T(1024)(128)(4,1)}), s8[4194304]{0:T(1024)(128)(4,1)S(1)}, s32[]{:S(2)}) async-start(s8[6291456]{0:T(1024)(128)(4,1)} %bitcast.90), calls=%async_computation.2 | async-start | bytes 8388608
  79.0 4.4 %slice-start.1 = ((s8[6291456]{0:T(1024)(128)(4,1)}), s8[2097152]{0:T(1024)(128)(4,1)S(1)}, s32[]{:S(2)}) async-start(s8[6291456]{0:T(1024)(128)(4,1)} %bitcast.90), calls=%async_computation.3 | async-start | bytes 4194304
Sparse Core Ops, SparseCore 0:
  48.9 28.7 all-gather.3
where the time goes:
time: 99.4 us; the launch traced here: 99 us
  waiting for transfers between devices  23.1 us (23%)
  blocking collectives  22.7 us (23%)
  between operations  14.3 us (14%)
  matrix products  11.7 us (12%)
  local copies, waits for them, and re-layouts  10.9 us (11%)
  other arithmetic  10.1 us (10%)
  starting transfers between devices  6.32 us (6%)
    all_gather x1, waiting for transfers between devices, local(): gathered = lax.all_gather(compact, 'blk', axis=0, tiled=True)  23 us
    all_gather x1, blocking collectives, local(): new_all = lax.all_gather(kv_new.transpose(1, 0, 2), 'blk', axis=0)  22.7 us
    all_to_all x1, starting transfers between devices, local(): lax.all_to_all(sent_pages, 'blk', split_axis=0, concat_axis=0, tiled=True)  6.32 us
    dot_general x2, matrix products, attend(): jnp.einsum('gqd,gkd->gqk', queries, keys, preferred_element_type=jnp.floa...  5.92 us
    dot_general x2, matrix products, attend(): jnp.einsum('gqk,gkd->gqd', weights.astype(jnp.bfloat16), values, preferre...  5.77 us
    reduce_sum x2, other arithmetic, attend(): totals = totals * factor + jnp.sum(weights, axis=2)  4.12 us
    gather x1, local copies, waits for them, and re-layouts, local(): kv_cache[chosen]  3.56 us
    unnamed x7, local copies, waits for them, and re-layouts  3.01 us
  transfers between devices with their start and end apart: 2, of which 1 were waited for; matrix products, arithmetic and copies ran while one was open for 9% of the time, Pallas kernels for 0%

commit v1 on v0

--- a/solution.py
+++ b/solution.py
@@ -76,7 +76,12 @@
     )
     compact = page_part[positions]
     compact_valid = jnp.arange(pg, dtype=jnp.int32) * blocks + myself < npages
-    gathered = lax.all_gather(compact, "blk", axis=0, tiled=True)
+    ring = [compact]
+    for hop in range(3):
+        ring.append(lax.ppermute(ring[-1], "blk", [(dev, (dev + 1) % 4) for dev in range(4)]))
+    gathered = jnp.roll(
+        jnp.concatenate(ring[::-1], axis=0), (lax.axis_index("blk") + 1) * ring[0].shape[0], axis=0
+    )
     gathered_valid = (
         jnp.arange(pg, dtype=jnp.int32)[None, :] * blocks + block_ids[:, None] < npages
     ).reshape(-1)

time: 99.4 us -> 84.5 us (0.85)
  between operations: 14.3 us -> 0.96 us
  waiting for transfers between devices: 23.1 us -> 27.9 us
  local copies, waits for them, and re-layouts: 10.9 us -> 8.24 us
  matrix products: 11.7 us -> 9.36 us
  blocking collectives: 22.7 us -> 21.1 us
    all_gather x1 -> x0, waiting for transfers between devices: 23 us -> none  [local(): gathered = lax.all_gather(compact, 'blk', axis=0, tiled=True)]
    ppermute x0 -> x3, waiting for transfers between devices: none -> 16.4 us  [local(): lax.ppermute(ring[-1], 'blk', [(dev, (dev + 1) % 4) for dev in range(4)])]
    all_to_all x1, waiting for transfers between devices: 0.01 us -> 11.5 us  [local(): lax.all_to_all(sent_pages, 'blk', split_axis=0, concat_axis=0, tiled=True)]
    dot_general x2, matrix products: 5.92 us -> 3.27 us  [attend(): jnp.einsum('gqd,gkd->gqk', queries, keys, preferred_element_type=jnp.floa...]
    all_gather x1, blocking collectives: 22.7 us -> 21.1 us  [local(): new_all = lax.all_gather(kv_new.transpose(1, 0, 2), 'blk', axis=0)]
    transpose x1 -> x2, local copies, waits for them, and re-layouts: 1.29 us -> 0.18 us  [local(): gathered.transpose(1, 0, 2, 3)]
    unnamed x7 -> x10, local copies, waits for them, and re-layouts: 3.01 us -> 3.14 us
  transfers between devices with their start and end apart: 2 -> 4, of which waited for: 1 -> 3; matrix products, arithmetic and copies ran while one was open for 9% -> 7% of each run, Pallas kernels for 0% -> 0%
where the time goes in v1:
time: 84.5 us; the launch traced here: 84.2 us
  waiting for transfers between devices  27.9 us (33%)
  blocking collectives  21.1 us (25%)
  other arithmetic  10.2 us (12%)
  matrix products  9.36 us (11%)
  local copies, waits for them, and re-layouts  8.24 us (10%)
  starting transfers between devices  6.44 us (8%)
  between operations  0.96 us (1%)
    all_gather x1, blocking collectives, local(): new_all = lax.all_gather(kv_new.transpose(1, 0, 2), 'blk', axis=0)  21.1 us
    ppermute x3, waiting for transfers between devices, local(): lax.ppermute(ring[-1], 'blk', [(dev, (dev + 1) % 4) for dev in range(4)])  16.4 us
    all_to_all x1, waiting for transfers between devices, local(): lax.all_to_all(sent_pages, 'blk', split_axis=0, concat_axis=0, tiled=True)  11.5 us
    all_to_all x1, starting transfers between devices, local(): lax.all_to_all(sent_pages, 'blk', split_axis=0, concat_axis=0, tiled=True)  6.32 us
    dot_general x2, matrix products, attend(): jnp.einsum('gqk,gkd->gqd', weights.astype(jnp.bfloat16), values, preferre...  6.09 us
    reduce_sum x2, other arithmetic, attend(): totals = totals * factor + jnp.sum(weights, axis=2)  4.19 us
    gather x1, local copies, waits for them, and re-layouts, local(): kv_cache[chosen]  3.56 us
    dot_general x2, matrix products, attend(): jnp.einsum('gqd,gkd->gqk', queries, keys, preferred_element_type=jnp.floa...  3.27 us
  transfers between devices with their start and end apart: 4, of which 3 were waited for; matrix products, arithmetic and copies ran while one was open for 7% of the time, Pallas kernels for 0%

profile of v1, /device:TPU:0, one launch (start us, length us, event | category | flops | bytes accessed | tf_op | source)
XLA Modules:
  0.0 84.2 jit_solution(504096796173088529)
XLA Ops:
  0.0 0.7 and_select_fusion.3
  0.7 0.7 convert_bitcast_fusion
  1.8 1.4 %fusion.35 = (s32[]{:T(128)}, s32[]{:T(128)}) fusion(s32[4]{0:T(128)} %param.9, s32[]{:T(128)S(6)} %axis_index.19, s32[4]{0:T(128)S(1)} %convert_reduce_fusion, s32[4,1]{0,1:T(1,128)S(1)} %reduce-window.22), kind=kLoop, calls=%fused_computation.86 | loop fusion | flops 22 | bytes 60 | tf_op jit(solution)/shard_map/reduce_sum | solution.py:39
  3.2 0.7 and_select_fusion.4
  4.1 3.6 %gather_fusion = bf16[4,2,128,256]{3,2,1,0:T(8,128)(2,1)} fusion(bf16[32,2,128,256]{3,2,1,0:T(8,128)(2,1)} %param.7, s32[1024]{0:T(1024)S(1)} %pad_clamp_fusion.1), kind=kCustom, calls=%fused_computation | custom fusion | bytes 1048592 | tf_op jit(solution)/shard_map/gather | solution.py:60
  7.6 6.3 %all-to-all-start = ((bf16[4,2,128,256]{3,2,1,0:T(8,128)(2,1)}), bf16[4,2,128,256]{3,2,1,0:T(8,128)(2,1)S(1)}, u32[]{:S(2)}, u32[]{:S(2)}) async-start(bf16[4,2,128,256]{3,2,1,0:T(8,128)(2,1)} %gather_fusion), calls=%async_computation | async-start | bytes 1048576 | tf_op jit(solution)/shard_map/all_to_all | solution.py:64
  15.2 0.9 %copy.36 = bf16[128,2,256]{2,0,1:T(8,128)(2,1)S(1)} copy(bf16[128,2,256]{2,1,0:T(2,128)(2,1)} %param.6) | data formatting | bytes 262144 | tf_op args[1]
  16.1 0.7 select_reduce_fusion
  16.9 11.5 %all-to-all-done = bf16[4,2,128,256]{3,2,1,0:T(8,128)(2,1)S(1)} async-done(((bf16[4,2,128,256]{3,2,1,0:T(8,128)(2,1)}), bf16[4,2,128,256]{3,2,1,0:T(8,128)(2,1)S(1)}, u32[]{:S(2)}, u32[]{:S(2)}) %all-to-all-start) | async-done | bytes 524320 | tf_op jit(solution)/shard_map/all_to_all | solution.py:64
  28.4 0.6 gather_fusion.1
  29.1 21.1 %all-gather = bf16[8,128,256]{2,1,0:T(8,128)(2,1)S(1)} all-gather(bf16[2,128,256]{2,1,0:T(8,128)(2,1)S(1)} %bitcast.99), channel_id=2, replica_groups=mesh['groups'=2,'blk'=4,'pool'=4] {'blk'}, dimensions={0}, use_global_device_ids=true | all-gather | bytes 655360 | tf_op jit(solution)/shard_map/all_gather | solution.py:47
  50.2 1.1 %copy.31 = bf16[16,8,16,128]{3,2,1,0:T(8,128)(2,1)S(1)} copy(bf16[16,8,16,128]{3,1,2,0:T(8,128)(2,1)} %bitcast.100) | data formatting | bytes 1048576
  51.5 0.4 broadcast_compare_fusion
  52.0 0.4 pad_add_fusion
  52.4 9.7 %collective-permute-done.1 = bf16[2,2,128,256]{3,2,1,0:T(8,128)(2,1)S(1)} collective-permute-done((bf16[2,2,128,256]{3,2,1,0:T(8,128)(2,1)S(1)}, bf16[2,2,128,256]{3,2,1,0:T(8,128)(2,1)S(1)}, u32[]{:S(2)}, u32[]{:S(2)}) %collective-permute-start.1) | collective-permute-done | bytes 262176 | tf_op jit(solution)/shard_map/ppermute | solution.py:81
  62.1 1.4 %fusion.4 = (f32[2,1024]{1,0:T(2,128)S(1)}, f32[2,768,1024]{2,1,0:T(8,128)S(1)}) fusion(pred[1024,768]{0,1:T(8,128)(4,1)S(1)} %pad_add_fusion, bf16[2,1024,128]{2,1,0:T(8,128)(2,1)S(1)} %bitcast.94, bf16[2,512,256]{2,1,0:T(8,128)(2,1)S(1)} %bitcast.101, bf16[2,256,256]{2,1,0:T(8,128)(2,1)S(1)} %bitcast.104), kind=kOutput, calls=%fused_computation.11 | convolution fusion | flops 408156160 | bytes 8396800 | tf_op jit(solution)/shard_map/gqd,gkd->gqk/dot_general | solution.py:14
  63.5 6.8 %collective-permute-done.2 = bf16[2,2,128,256]{3,2,1,0:T(8,128)(2,1)S(1)} collective-permute-done((bf16[2,2,128,256]{3,2,1,0:T(8,128)(2,1)S(1)}, bf16[2,2,128,256]{3,2,1,0:T(8,128)(2,1)S(1)}, u32[]{:S(2)}, u32[]{:S(2)}) %collective-permute-start.2) | collective-permute-done | bytes 262176 | tf_op jit(solution)/shard_map/ppermute | solution.py:81
  70.7 1.9 %bitcast_reduce_fusion = (f32[2,1024]{1,0:T(2,128)S(1)}, f32[2,1024,1024]{2,1,0:T(8,128)S(1)}) fusion(pred[1024]{0:T(1024)(128)(4,1)S(1)} %broadcast_bitcast_fusion.1, bf16[2,1024,128]{2,1,0:T(8,128)(2,1)S(1)} %bitcast.95, bf16[2,1024,256]{2,1,0:T(8,128)(2,1)S(1)} %bitcast.92), kind=kOutput, calls=%fused_computation.3 | convolution fusion | flops 543160320 | bytes 9446400 | tf_op jit(solution)/shard_map/gqd,gkd->gqk/dot_general | solution.py:14
  72.6 2.5 %fusion.2 = f32[2,1024]{1,0:T(2,128)S(1)} fusion(f32[2,1024,1024]{2,1,0:T(8,128)S(1)} %get-tuple-element.16, f32[2,1024]{1,0:T(2,128)S(1)} %get-tuple-element.11, pred[1024]{0:T(1024)(128)(4,1)S(1)} %broadcast_bitcast_fusion.1), kind=kLoop, calls=%fused_computation.9 | loop fusion | flops 10483712 | bytes 8406016 | tf_op jit(solution)/shard_map/reduce_sum | solution.py:20
  75.1 1.7 %fusion.5 = f32[2,1024]{1,0:T(2,128)S(1)} fusion(f32[2,768,1024]{2,1,0:T(8,128)S(1)} %get-tuple-element.14, f32[2,1024]{1,0:T(2,128)S(1)} %get-tuple-element.12, pred[1024,768]{0,1:T(8,128)(4,1)S(1)} %pad_add_fusion), kind=kLoop, calls=%fused_computation.12 | loop fusion | flops 7862272 | bytes 7094272 | tf_op jit(solution)/shard_map/reduce_sum | solution.py:20
  76.8 2.9 %fusion.20 = f32[2,1024,128]{2,1,0:T(8,128)S(1)} fusion(f32[2,768,1024]{2,1,0:T(8,128)S(1)} %get-tuple-element.14, f32[2,1024]{1,0:T(2,128)S(1)} %get-tuple-element.12, pred[1024,768]{0,1:T(8,128)(4,1)S(1)} %pad_add_fusion, f32[2,1024]{1,0:T(2,128)S(1)} %get-tuple-element.6, f32[2,1024]{1,0:T(2,128)S(1)} %get-tuple-element.10, ...), kind=kOutput, calls=%fused_computation.22 | convolution fusion | flops 411828224 | bytes 8937472 | tf_op jit(solution)/shard_map/gqk,gkd->gqd/dot_general | solution.py:21
  79.8 3.1 %divide_convert_fusion = bf16[2,1024,128]{2,1,0:T(8,128)(2,1)S(1)} fusion(f32[2,1024,128]{2,1,0:T(8,128)S(1)} %fusion.20, f32[2,1024,1024]{2,1,0:T(8,128)S(1)} %get-tuple-element.16, f32[2,1024]{1,0:T(2,128)S(1)} %get-tuple-element.11, pred[1024]{0:T(1024)(128)(4,1)S(1)} %broadcast_bitcast_fusion.1, bf16[2,1024,256]{2,1,0:T(8,128)(2,1)S(1)} %bitcast.93, ...), kind=kOutput, calls=%fused_computation.23 | convolution fusion | flops 548143104 | bytes 10504192 | tf_op jit(solution)/shard_map/gqk,gkd->gqd/dot_general | solution.py:21
  82.9 0.3 copy.28
  83.3 0.9 %copy.35 = bf16[16,8,16,128]{3,1,2,0:T(8,128)(2,1)} copy(bf16[16,8,16,128]{3,2,1,0:T(8,128)(2,1)S(1)} %bitcast.97) | data formatting | bytes 1048576
  (44 shorter events, 2.0 us)
Async XLA Ops:
  7.6 20.8 %all-to-all-start = ((bf16[4,2,128,256]{3,2,1,0:T(8,128)(2,1)}), bf16[4,2,128,256]{3,2,1,0:T(8,128)(2,1)S(1)}, u32[]{:S(2)}, u32[]{:S(2)}) async-start(bf16[4,2,128,256]{3,2,1,0:T(8,128)(2,1)} %gather_fusion), calls=%async_computation | async-start | bytes 1048576 | tf_op jit(solution)/shard_map/all_to_all | solution.py:64
  29.0 22.9 %collective-permute-start = (bf16[2,2,128,256]{3,2,1,0:T(8,128)(2,1)S(1)}, bf16[2,2,128,256]{3,2,1,0:T(8,128)(2,1)S(1)}, u32[]{:S(2)}, u32[]{:S(2)}) collective-permute-start(bf16[2,2,128,256]{3,2,1,0:T(8,128)(2,1)S(1)} %gather_fusion.1), channel_id=1, source_target_pairs={{0,4},{4,8},{8,12},{12,0},{1,5},{5,9},{9,13},{13,1},{2,6},{6,10},{... | collective-permute-start | bytes 786440 | tf_op jit(solution)/shard_map/ppermute | solution.py:81
  51.9 10.2 %collective-permute-start.1 = (bf16[2,2,128,256]{3,2,1,0:T(8,128)(2,1)S(1)}, bf16[2,2,128,256]{3,2,1,0:T(8,128)(2,1)S(1)}, u32[]{:S(2)}, u32[]{:S(2)}) collective-permute-start(bf16[2,2,128,256]{3,2,1,0:T(8,128)(2,1)S(1)} %collective-permute-done), channel_id=1, source_target_pairs={{0,4},{4,8},{8,12},{12,0},{1,5},{5,9},{9,13},{13,1},{2,6},{6,10},{... | collective-permute-start | bytes 786440 | tf_op jit(solution)/shard_map/ppermute | solution.py:81
  62.1 8.2 %collective-permute-start.2 = (bf16[2,2,128,256]{3,2,1,0:T(8,128)(2,1)S(1)}, bf16[2,2,128,256]{3,2,1,0:T(8,128)(2,1)S(1)}, u32[]{:S(2)}, u32[]{:S(2)}) collective-permute-start(bf16[2,2,128,256]{3,2,1,0:T(8,128)(2,1)S(1)} %collective-permute-done.1), channel_id=1, source_target_pairs={{0,4},{4,8},{8,12},{12,0},{1,5},{5,9},{9,13},{13,1},{2,6},{6,10},{... | collective-permute-start | bytes 786440 | tf_op jit(solution)/shard_map/ppermute | solution.py:81
